TPU v7x, 512 devices: a whole 4x8x8 slice. The times are simulated.
512 devices in a mesh: grp: 16 (over z, core), dev: 32 (over x, y).
Axes of the slice: x: 4, y: 8, z: 8, core: 2. Of those that a mesh axis runs over, the one named last changes fastest.
Arguments:
- ssm_input: bfloat16 [4096, 4096], P('grp', 'dev'), may hold values from -6 to 6
- gate_input: bfloat16 [4096, 4096], P('grp', 'dev'), may hold values from -6 to 6
- step_size: float32 [4096, 64], P('grp', 'dev'), may hold values from 6.1035156e-05 to 0.3375
- decay_rate: float32 [64], P('dev'), may hold values from 0.5 to 2
- in_coeff: bfloat16 [4096, 128], P('grp'), may hold values from -6 to 6
- out_coeff: bfloat16 [4096, 128], P('grp'), may hold values from -6 to 6
- skip_gain: float32 [64], P('dev'), may hold values from 0.5 to 3
- norm_gain: float32 [4096], P('dev'), may hold values from 0.5 to 1.5
- out_proj: bfloat16 [4096, 2048], P(None, 'dev'), may hold values from -0.09375 to 0.09375
- residual: bfloat16 [4096, 2048], P(('grp', 'dev')), may hold values from -6 to 6
- ffn_gain: float32 [2048], replicated, may hold values from 0.5 to 1.5
- router: float32 [2048, 16], replicated, may hold values from -0.125 to 0.125
- routes: int32 [4096, 2], P(('grp', 'dev')), may hold values from 0 to 15, all different within a row; in each aligned block of 8 rows (0 to 7, 8 to 15, ...) at most 2 rows name the same one
- gate_weight: bfloat16 [16, 2048, 8192], P('grp', None, 'dev'), may hold values from -0.125 to 0.125
- up_weight: bfloat16 [16, 2048, 8192], P('grp', None, 'dev'), may hold values from -0.125 to 0.125
- down_weight: bfloat16 [16, 8192, 2048], P('grp', 'dev'), may hold values from -0.0625 to 0.0625
Outputs:
- moe_out: bfloat16 [4096, 2048], P(('grp', 'dev'))
Inputs may be any that keep to these rules, and one draw needn't show every extreme that they name: `routes`: each row names two different experts; among the 8 rows of one dispatch block of consecutive tokens no expert is named more than 2 times, a bound that some block reaches.
All inputs are finite; a program needn't handle non-finite values.
Results may differ from a plain program's by a relative error of at most 0.012.
Values may be sent and summed in bfloat16 or wider, within the bound.
No kernel may reach another device: no remote copies, remote signals or barrier semaphores. Data moves between devices by JAX's collectives and lax.ppermute only.
A program may use at most 64 MiB of HBM per device.

v0:
```python
import jax
import jax.numpy as jnp
from jax import lax
from jax.sharding import Mesh
from jax.sharding import PartitionSpec as P

DEV = ("dev_0", "dev_1")
GRP_DEV = ("grp", "dev_0", "dev_1")
EPSILON = 1e-05
HIGHEST_PREC = lax.Precision.HIGHEST


def side_by_side(arrays, axis, dim, along):
    columns = [a.reshape(*a.shape[:along], -1) for a in arrays]
    both = jnp.concatenate(columns, axis=along)
    filled, at, finished = (lax.all_gather(both, axis, axis=dim, tiled=True), 0, [])
    for a, column in zip(arrays, columns):
        piece = filled[..., at : at + column.shape[along]]
        finished.append(piece.reshape(*piece.shape[:along], *a.shape[along:]))
        at += column.shape[along]
    return tuple(finished)


def sent_to_all(shard, axis):
    peers = lax.axis_size(axis)
    return lax.all_to_all(
        jnp.broadcast_to(shard[None], (peers, *shard.shape)), axis, 0, 0, tiled=True
    )


def of_everyone(shard, axis):
    everything = sent_to_all(shard, axis)
    return jnp.sum(everything, axis=0)


def in_order(tiles, dim):
    dims = list(tiles.shape[1:])
    dims[dim] *= tiles.shape[0]
    return jnp.moveaxis(tiles, 0, dim).reshape(dims)


def collect(shard, axis, dim):
    return in_order(sent_to_all(shard, axis), dim)


def sum_by_axis(terms, axes):
    total = terms.astype(jnp.bfloat16)
    for axis in axes:
        total = lax.psum_scatter(total, axis, scatter_dimension=0, tiled=True)
    return total.astype(jnp.float32)


def rms_scale(values, gain_vec):
    return (
        values * lax.rsqrt(jnp.mean(values * values, axis=-1, keepdims=True) + EPSILON) * gain_vec
    )


def slot_tables(routes_block, expert_count, slot_cap):
    blocks, row_total = (routes_block.shape[0], routes_block.shape[1])
    flat_routes = routes_block.reshape(blocks, row_total * 2)
    onehot = (
        flat_routes[:, :, None] == jnp.arange(expert_count, dtype=jnp.int32)[None, None, :]
    ).astype(jnp.int32)
    earlier = jnp.cumsum(onehot, axis=1) - onehot
    slot_rank = jnp.sum(earlier * onehot, axis=2)
    slot_index = (flat_routes * slot_cap + slot_rank).reshape(blocks, row_total, 2)
    placed = (
        slot_index[:, :, :, None]
        == jnp.arange(expert_count * slot_cap, dtype=jnp.int32)[None, None, None, :]
    )
    return placed.astype(jnp.float32)


def shards(
    ssm_input,
    gate_input,
    step_size,
    decay_rate,
    in_coeff,
    out_coeff,
    skip_gain,
    norm_gain,
    out_proj,
    residual,
    ffn_gain,
    router,
    routes,
    gate_weight,
    up_weight,
    down_weight,
):
    tok_rows = ssm_input.shape[0]
    head_count = step_size.shape[1]
    head_width = ssm_input.shape[1] // head_count
    dev_count = lax.axis_size(DEV)
    inner_dim = ssm_input.shape[1] * dev_count
    block_rows = residual.shape[0]
    model_dim = residual.shape[1]
    experts = lax.axis_size("grp")
    slot_cap = max(2, 4 * block_rows // experts)
    group_slots = experts * slot_cap
    inputs_f = ssm_input.astype(jnp.float32).reshape(tok_rows, head_count, head_width)
    in_float = in_coeff.astype(jnp.float32)
    out_float = out_coeff.astype(jnp.float32)
    log_rate = -(step_size * decay_rate[None, :])
    cumulative = jnp.cumsum(log_rate, axis=0)
    causal = (jnp.arange(tok_rows)[:, None] >= jnp.arange(tok_rows)[None, :])[:, :, None]
    spread = cumulative[:, None, :] - cumulative[None, :, :]
    decay_pair = jnp.where(causal, jnp.exp(jnp.where(causal, spread, 0.0)), 0.0)
    scores = jnp.dot(out_coeff, in_coeff.T, preferred_element_type=jnp.float32)
    mixing = decay_pair * scores[:, :, None] * step_size[None, :, :]
    inside = jnp.einsum("tuh,uhp->thp", mixing, inputs_f, precision=HIGHEST_PREC)
    to_end = jnp.exp(cumulative[-1][None, :] - cumulative) * step_size
    own_state = jnp.einsum("uh,uhp,un->hpn", to_end, inputs_f, in_float, precision=HIGHEST_PREC)
    own_log = cumulative[-1]
    group_logs, group_states = tuple(
        (
            part.astype(jnp.float32)
            for part in side_by_side(
                (own_log[None].astype(jnp.bfloat16), own_state[None].astype(jnp.bfloat16)),
                "grp",
                0,
                2,
            )
        )
    )
    group_index = jnp.arange(group_logs.shape[0])
    my_group = lax.axis_index("grp")
    inclusive = jnp.cumsum(group_logs, axis=0)
    exclusive = inclusive - group_logs
    before_me = jnp.sum(jnp.where((group_index == my_group)[:, None], exclusive, 0.0), axis=0)
    earlier_mask = (group_index < my_group)[:, None]
    weighting = jnp.where(
        earlier_mask, jnp.exp(jnp.where(earlier_mask, before_me[None, :] - inclusive, 0.0)), 0.0
    )
    entering = jnp.einsum("gh,ghpn->hpn", weighting, group_states, precision=HIGHEST_PREC)
    carried = jnp.exp(cumulative)[:, :, None] * jnp.einsum(
        "hpn,tn->thp", entering, out_float, precision=HIGHEST_PREC
    )
    ssm_out = inside + carried + skip_gain[None, :, None] * inputs_f
    gated_out = ssm_out.reshape(tok_rows, head_count * head_width) * jax.nn.silu(
        gate_input.astype(jnp.float32)
    )
    squares = of_everyone(jnp.sum(gated_out * gated_out, axis=1), DEV)
    mixed_rows = (
        gated_out * lax.rsqrt(squares[:, None] / inner_dim + EPSILON) * norm_gain[None, :]
    ).astype(jnp.bfloat16)
    projected = jnp.dot(
        collect(mixed_rows, DEV, 1), out_proj, preferred_element_type=jnp.float32
    ).astype(jnp.bfloat16)
    mamba_out = lax.all_to_all(projected, DEV, split_axis=0, concat_axis=1, tiled=True)
    hidden_res = (residual.astype(jnp.float32) + mamba_out.astype(jnp.float32)).astype(jnp.bfloat16)
    hidden_float = hidden_res.astype(jnp.float32)
    normed = rms_scale(hidden_float, ffn_gain).astype(jnp.bfloat16)
    logits = jnp.dot(normed.astype(jnp.float32), router, precision=HIGHEST_PREC)
    expert_ids = jnp.arange(experts, dtype=jnp.int32)[None, :]
    first_logit = jnp.sum(logits * (routes[:, 0:1] == expert_ids).astype(jnp.float32), axis=1)
    second_logit = jnp.sum(logits * (routes[:, 1:2] == expert_ids).astype(jnp.float32), axis=1)
    first_prob = jax.nn.sigmoid(first_logit - second_logit)
    second_prob = 1.0 - first_prob
    placed = slot_tables(routes[None], experts, slot_cap)[0]
    filled = jnp.sum(placed, axis=1)
    outgoing = jnp.dot(
        filled.T.astype(jnp.bfloat16), normed, preferred_element_type=jnp.float32
    ).astype(jnp.bfloat16)
    outgoing = outgoing.reshape(experts, slot_cap, model_dim)
    arrived = lax.all_to_all(outgoing, "grp", split_axis=0, concat_axis=0, tiled=True)
    all_rows = lax.all_gather(arrived, DEV, axis=0, tiled=True).reshape(-1, model_dim)
    gate_act = jnp.dot(all_rows, gate_weight[0], preferred_element_type=jnp.float32)
    up_act = jnp.dot(all_rows, up_weight[0], preferred_element_type=jnp.float32)
    hidden = (jax.nn.silu(gate_act) * up_act).astype(jnp.bfloat16)
    summed = sum_by_axis(jnp.dot(hidden, down_weight[0], preferred_element_type=jnp.float32), DEV)
    returned = lax.all_to_all(
        summed.astype(jnp.bfloat16).reshape(experts, slot_cap, model_dim),
        "grp",
        split_axis=0,
        concat_axis=0,
        tiled=True,
    )
    weights = first_prob[:, None] * placed[:, 0, :] + second_prob[:, None] * placed[:, 1, :]
    contrib = jnp.dot(
        weights,
        returned.reshape(group_slots, model_dim).astype(jnp.float32),
        precision=HIGHEST_PREC,
    )
    return (hidden_float + contrib).astype(jnp.bfloat16)


def solution(mesh):
    torus = Mesh(mesh.devices.reshape(mesh.shape["grp"], 4, 8), ("grp", "dev_0", "dev_1"))
    in_specs = (
        P("grp", DEV),
        P("grp", DEV),
        P("grp", DEV),
        P(DEV),
        P("grp", None),
        P("grp", None),
        P(DEV),
        P(DEV),
        P(None, DEV),
        P(GRP_DEV, None),
        P(),
        P(),
        P(GRP_DEV, None),
        P("grp", None, DEV),
        P("grp", None, DEV),
        P("grp", DEV, None),
    )
    out_specs = P(GRP_DEV, None)
    return jax.shard_map(
        shards, mesh=torus, in_specs=in_specs, out_specs=out_specs, check_vma=False
    )
```

profile of v0, /device:TPU:1, one launch (start us, length us, event | category | flops | bytes accessed | tf_op | source)
XLA Modules:
  0.0 366.3 jit_solution(13563389187455256031)
XLA Ops:
  6.6 0.9 negate_bitcast_fusion
  8.7 0.9 copy.73
  9.7 0.8 fusion.55
  10.4 1.0 convolution_convert_fusion.2
  11.6 26.0 %all_gather.6 = bf16[16,2,8193]{2,1,0:T(2,128)(2,1)S(1)} all-gather(bf16[1,2,8193]{2,1,0:T(2,128)(2,1)S(1)} %pad_maximum_fusion), channel_id=1, replica_groups=mesh['grp'=16,'dev_0'=4,'dev_1'=8] {'grp'}, dimensions={0}, use_global_device_ids=true | all-gather | bytes 557124 | tf_op jit(solution)/shard_map/all_gather | solution.py:16
  39.2 1.1 fusion.56
  42.0 18.2 %all_to_all.34 = f32[32,1,256]{2,1,0:T(1,128)S(1)} all-to-all(f32[32,1,256]{2,1,0:T(1,128)S(1)} %broadcast_in_dim.80), channel_id=1, replica_groups=mesh['grp'=16,'dev_0'=4,'dev_1'=8] {'dev_0','dev_1'}, dimensions={0} | all-to-all | bytes 65536 | tf_op jit(solution)/shard_map/all_to_all | solution.py:26
  60.5 1.6 broadcast_in_dim.81
  62.1 4.1 %all-to-all-start.1 = ((bf16[32,256,128]{1,2,0:T(8,128)(2,1)}), bf16[32,256,128]{1,2,0:T(8,128)(2,1)S(1)}, u32[]{:S(2)}, u32[]{:S(2)}) async-start(bf16[32,256,128]{1,2,0:T(8,128)(2,1)} %broadcast_in_dim.81), calls=%async_computation.1 | async-start | bytes 4194304 | tf_op jit(solution)/shard_map/all_to_all | solution.py:26
  66.9 48.6 %all-to-all-done.1 = bf16[32,256,128]{1,2,0:T(8,128)(2,1)S(1)} async-done(((bf16[32,256,128]{1,2,0:T(8,128)(2,1)}), bf16[32,256,128]{1,2,0:T(8,128)(2,1)S(1)}, u32[]{:S(2)}, u32[]{:S(2)}) %all-to-all-start.1) | async-done | bytes 2097184 | tf_op jit(solution)/shard_map/all_to_all | solution.py:26
  115.5 1.5 convolution_convert_fusion.3
  117.9 6.4 %all-to-all-start.2 = ((bf16[32,2,256]{2,1,0:T(2,128)(2,1)}), bf16[32,2,256]{2,1,0:T(2,128)(2,1)S(1)}, u32[]{:S(2)}, u32[]{:S(2)}) async-start(bf16[32,2,256]{2,1,0:T(2,128)(2,1)} %reshape.260), calls=%async_computation.2 | async-start | bytes 65536 | tf_op jit(solution)/shard_map/all_to_all | solution.py:152
  124.4 8.6 %all-to-all-done.2 = bf16[32,2,256]{2,1,0:T(2,128)(2,1)S(1)} async-done(((bf16[32,2,256]{2,1,0:T(2,128)(2,1)}), bf16[32,2,256]{2,1,0:T(2,128)(2,1)S(1)}, u32[]{:S(2)}, u32[]{:S(2)}) %all-to-all-start.2) | async-done | bytes 32800 | tf_op jit(solution)/shard_map/all_to_all | solution.py:152
  133.8 14.9 %all_to_all.35 = bf16[16,2,2048]{2,1,0:T(2,128)(2,1)} all-to-all(bf16[16,2,2048]{2,1,0:T(2,128)(2,1)S(1)} %reshape.248), channel_id=1, replica_groups=mesh['grp'=16,'dev_0'=4,'dev_1'=8] {'grp'}, dimensions={0} | all-to-all | bytes 262144 | tf_op jit(solution)/shard_map/all_to_all | solution.py:168
  148.8 73.9 %all-gather.2.cloned.1.call-done = bf16[512,2,2048]{2,1,0:T(2,128)(2,1)} async-done(((bf16[16,2,2048]{2,1,0:T(2,128)(2,1)}), bf16[512,2,2048]{2,1,0:T(2,128)(2,1)}) %all-gather.2.cloned.1.call-update) | async-done | bytes 4194320 | tf_op jit(solution)/shard_map/all_gather | solution.py:169
  222.7 7.2 %reshape.249 = bf16[1024,2048]{1,0:T(8,128)(2,1)} reshape(bf16[512,2,2048]{2,1,0:T(2,128)(2,1)} %all-gather.2.cloned.1.call-done) | data formatting | bytes 8388608 | tf_op jit(solution)/shard_map/reshape | solution.py:169
  229.9 4.5 %fusion.8 = f32[1024,256]{1,0:T(8,128)} fusion(bf16[1024,2048]{1,0:T(8,128)(2,1)} %reshape.249, bf16[1,2048,256]{2,1,0:T(8,128)(2,1)S(1)} %copy-done.8), kind=kOutput, calls=%fused_computation.15 | convolution fusion | flops 1073741824 | bytes 6291456 | tf_op jit(solution)/shard_map/dot_general | solution.py:170
  234.4 9.1 %convolution_convert_fusion = bf16[1024,2048]{1,0:T(8,128)(2,1)} fusion(bf16[1024,2048]{1,0:T(8,128)(2,1)} %reshape.249, bf16[1,256,2048]{2,1,0:T(8,128)(2,1)S(1)} %copy-done, bf16[1,2048,256]{2,1,0:T(8,128)(2,1)} %param.30, f32[1024,256]{1,0:T(8,128)} %fusion.8), kind=kOutput, calls=%fused_computation | convolution fusion | flops 2151153664 | bytes 11534336 | tf_op jit(solution)/shard_map/dot_general | solution.py:173
  243.6 52.5 %reduce-scatter.3.cloned.1.call-done = bf16[256,2048]{1,0:T(8,128)(2,1)} async-done(((bf16[1024,2048]{1,0:T(8,128)(2,1)}), bf16[256,2048]{1,0:T(8,128)(2,1)}) %reduce-scatter.3.cloned.1.call-update) | async-done | bytes 1048592 | tf_op jit(solution)/shard_map/reduce_scatter | solution.py:49
  296.2 39.4 %reduce-scatter.5.cloned.1.call-done = bf16[32,2048]{1,0:T(8,128)(2,1)} async-done(((bf16[256,2048]{1,0:T(8,128)(2,1)}), bf16[32,2048]{1,0:T(8,128)(2,1)}) %reduce-scatter.5.cloned.1.call-update) | async-done | bytes 131088 | tf_op jit(solution)/shard_map/reduce_scatter | solution.py:49
  335.6 1.6 reshape.250
  337.2 12.5 %all-to-all-start.4 = ((bf16[16,2,2048]{2,1,0:T(2,128)(2,1)}), bf16[16,2,2048]{2,1,0:T(2,128)(2,1)S(1)}, u32[]{:S(2)}, u32[]{:S(2)}) async-start(bf16[16,2,2048]{2,1,0:T(2,128)(2,1)} %reshape.250), calls=%async_computation.6 | async-start | bytes 262144 | tf_op jit(solution)/shard_map/all_to_all | solution.py:174
  350.1 8.8 %all-to-all-done.4 = bf16[16,2,2048]{2,1,0:T(2,128)(2,1)S(1)} async-done(((bf16[16,2,2048]{2,1,0:T(2,128)(2,1)}), bf16[16,2,2048]{2,1,0:T(2,128)(2,1)S(1)}, u32[]{:S(2)}, u32[]{:S(2)}) %all-to-all-start.4) | async-done | bytes 131104 | tf_op jit(solution)/shard_map/all_to_all | solution.py:174
  358.9 0.9 fusion
  (84 shorter events, 7.9 us)
Async XLA Ops:
  6.5 227.9 %copy-start = (bf16[1,256,2048]{2,1,0:T(8,128)(2,1)S(1)}, bf16[1,256,2048]{2,1,0:T(8,128)(2,1)}, u32[]{:S(2)}) copy-start(bf16[1,256,2048]{2,1,0:T(8,128)(2,1)} %param.31) | copy-start | bytes 3145732
  6.5 34.5 %copy-start.5 = (f32[256,2]{0,1:T(2,128)S(1)}, f32[256,2]{0,1:T(2,128)}, u32[]{:S(2)}) copy-start(f32[256,2]{0,1:T(2,128)} %param.18) | copy-start | bytes 6148
  6.5 34.3 %copy-start.2 = (bf16[256,128]{1,0:T(8,128)(2,1)S(1)}, bf16[256,128]{1,0:T(8,128)(2,1)}, u32[]{:S(2)}) copy-start(bf16[256,128]{1,0:T(8,128)(2,1)} %param.21) | copy-start | bytes 196612
  6.5 34.5 %copy-start.10 = (f32[2]{0:T(128)S(1)}, f32[2]{0:T(128)}, u32[]{:S(2)}) copy-start(f32[2]{0:T(128)} %param.22) | copy-start | bytes 28
  6.5 35.3 %copy-start.1 = (bf16[256,128]{1,0:T(8,128)(2,1)S(1)}, bf16[256,128]{1,0:T(8,128)(2,1)}, u32[]{:S(2)}) copy-start(bf16[256,128]{1,0:T(8,128)(2,1)} %param.17) | copy-start | bytes 196612
  6.5 53.7 %copy-start.7 = (f32[128]{0:T(128)S(1)}, f32[128]{0:T(128)}, u32[]{:S(2)}) copy-start(f32[128]{0:T(128)} %param.23) | copy-start | bytes 1540
  41.1 25.2 %copy-start.6 = (s32[8,2]{0,1:T(2,128)S(1)}, s32[8,2]{0,1:T(2,128)}, u32[]{:S(2)}) copy-start(s32[8,2]{0,1:T(2,128)} %param.28) | copy-start | bytes 196
  62.1 71.2 %copy-start.3 = (bf16[8,2048]{1,0:T(8,128)(2,1)S(1)}, bf16[8,2048]{1,0:T(8,128)(2,1)}, u32[]{:S(2)}) copy-start(bf16[8,2048]{1,0:T(8,128)(2,1)} %param.25) | copy-start | bytes 98308
  62.1 71.4 %copy-start.4 = (f32[2048]{0:T(1024)S(1)}, f32[2048]{0:T(1024)}, u32[]{:S(2)}) copy-start(f32[2048]{0:T(1024)} %param.26) | copy-start | bytes 24580
  62.1 53.4 %all-to-all-start.1 = ((bf16[32,256,128]{1,2,0:T(8,128)(2,1)}), bf16[32,256,128]{1,2,0:T(8,128)(2,1)S(1)}, u32[]{:S(2)}, u32[]{:S(2)}) async-start(bf16[32,256,128]{1,2,0:T(8,128)(2,1)} %broadcast_in_dim.81), calls=%async_computation.1 | async-start | bytes 4194304 | tf_op jit(solution)/shard_map/all_to_all | solution.py:26
  117.9 15.2 %all-to-all-start.2 = ((bf16[32,2,256]{2,1,0:T(2,128)(2,1)}), bf16[32,2,256]{2,1,0:T(2,128)(2,1)S(1)}, u32[]{:S(2)}, u32[]{:S(2)}) async-start(bf16[32,2,256]{2,1,0:T(2,128)(2,1)} %reshape.260), calls=%async_computation.2 | async-start | bytes 65536 | tf_op jit(solution)/shard_map/all_to_all | solution.py:152
  124.3 98.4 %all-gather.2.cloned.1.call-start = ((), (), s32[]{:S(2)}) async-start(), calls=%async_computation.7 | async-start | bytes 4325376 | tf_op jit(solution)/shard_map/all_gather | solution.py:169
  148.8 81.2 %copy-start.8 = (bf16[1,2048,256]{2,1,0:T(8,128)(2,1)S(1)}, bf16[1,2048,256]{2,1,0:T(8,128)(2,1)}, u32[]{:S(2)}) copy-start(bf16[1,2048,256]{2,1,0:T(8,128)(2,1)} %param.29) | copy-start | bytes 3145732
  148.8 147.3 %reduce-scatter.3.cloned.1.call-start = ((), (), s32[]{:S(2)}) async-start(), calls=%async_computation.8 | async-start | bytes 5242880 | tf_op jit(solution)/shard_map/reduce_scatter | solution.py:49
  243.5 106.1 %copy-start.9 = (f32[2048,16]{0,1:T(8,128)S(1)}, f32[2048,16]{0,1:T(8,128)}, u32[]{:S(2)}) copy-start(f32[2048,16]{0,1:T(8,128)} %param.27) | copy-start | bytes 393220
  243.6 92.0 %reduce-scatter.5.cloned.1.call-start = ((), (), s32[]{:S(2)}) async-start(), calls=%async_computation.9 | async-start | bytes 1179648 | tf_op jit(solution)/shard_map/reduce_scatter | solution.py:49
  337.2 21.6 %all-to-all-start.4 = ((bf16[16,2,2048]{2,1,0:T(2,128)(2,1)}), bf16[16,2,2048]{2,1,0:T(2,128)(2,1)S(1)}, u32[]{:S(2)}, u32[]{:S(2)}) async-start(bf16[16,2,2048]{2,1,0:T(2,128)(2,1)} %reshape.250), calls=%async_computation.6 | async-start | bytes 262144 | tf_op jit(solution)/shard_map/all_to_all | solution.py:174
Sparse Core Ops, SparseCore 0:
  148.9 73.7 all-gather.1
  243.7 52.3 reduce-scatter.2
  299.1 36.3 reduce-scatter.4
where the time goes:
time: 367 us; the launch traced here: 366 us
  waiting for transfers between devices  232 us (63%)
  blocking collectives  59.1 us (16%)
  starting transfers between devices  23.1 us (6%)
  matrix products  20.1 us (5%)
  local copies, waits for them, and re-layouts  15 us (4%)
  between operations  13.4 us (4%)
  other arithmetic  3.74 us (1%)
    reduce_scatter x2, waiting for transfers between devices, sum_by_axis(): total = lax.psum_scatter(total, axis, scatter_dimension=0, tiled=True)  91.8 us
    all_gather x1, waiting for transfers between devices, shards(): lax.all_gather(arrived, DEV, axis=0, tiled=True).reshape(-1, model_dim)  73.9 us
    all_to_all x1, waiting for transfers between devices, sent_to_all(): lax.all_to_all(jnp.broadcast_to(shard[None], (peers, *shard.shape)), axis...  48.6 us
    all_gather x1, blocking collectives, side_by_side(): lax.all_gather(both, axis, axis=dim, tiled=True)  26 us
    all_to_all x1, blocking collectives, sent_to_all(): lax.all_to_all(jnp.broadcast_to(shard[None], (peers, *shard.shape)), axis...  18.2 us
    all_to_all x1, blocking collectives, shards(): lax.all_to_all(outgoing, 'grp', split_axis=0, concat_axis=0, tiled=True)  14.9 us
    all_to_all x1, starting transfers between devices, shards(): lax.all_to_all(summed.astype(jnp.bfloat16).reshape(experts, slot_cap, mod...  12.5 us
    dot_general x1, matrix products, shards(): jnp.dot(hidden, down_weight[0], preferred_element_type=jnp.float32)  9.1 us
  transfers between devices with their start and end apart: 6, of which 6 were waited for; matrix products, arithmetic and copies ran while one was open for 0% of the time, Pallas kernels for 0%

commit v1 on v0

--- a/solution.py
+++ b/solution.py
@@ -166,7 +166,9 @@
     ).astype(jnp.bfloat16)
     outgoing = outgoing.reshape(experts, slot_cap, model_dim)
     arrived = lax.all_to_all(outgoing, "grp", split_axis=0, concat_axis=0, tiled=True)
-    all_rows = lax.all_gather(arrived, DEV, axis=0, tiled=True).reshape(-1, model_dim)
+    all_rows = jnp.concatenate(
+        lax.all_to_all(jnp.stack([arrived] * lax.axis_size(DEV)), DEV, 0, 0), axis=0
+    ).reshape(-1, model_dim)
     gate_act = jnp.dot(all_rows, gate_weight[0], preferred_element_type=jnp.float32)
     up_act = jnp.dot(all_rows, up_weight[0], preferred_element_type=jnp.float32)
     hidden = (jax.nn.silu(gate_act) * up_act).astype(jnp.bfloat16)

time: 367 us -> 388 us (1.057)
  blocking collectives: 59.1 us -> 157 us
  waiting for transfers between devices: 232 us -> 151 us
  local copies, waits for them, and re-layouts: 15 us -> 18.9 us
    all_to_all x0 -> x1, blocking collectives: none -> 99 us  [shards(): lax.all_to_all(jnp.stack([arrived] * lax.axis_size(DEV)), DEV, 0, 0)]
    all_gather x1 -> x0, waiting for transfers between devices: 73.9 us -> none  [shards(): lax.all_gather(arrived, DEV, axis=0, tiled=True).reshape(-1, model_dim)]
    another operation x0 -> x2, local copies, waits for them, and re-layouts: none -> 11.1 us  [the longest x1 7.3 us: shards(): all_rows = jnp.concatenate(lax.all_to_all(jnp.stack([arrived] * lax.axis_...]
    reduce_scatter x2, waiting for transfers between devices: 91.8 us -> 84.5 us  [sum_by_axis(): total = lax.psum_scatter(total, axis, scatter_dimension=0, tiled=True)]
    reshape x2 -> x1, local copies, waits for them, and re-layouts: 7.23 us -> 0.02 us  [the longest x1 7.21 us: shards(): lax.all_gather(arrived, DEV, axis=0, tiled=True).reshape(-1, model_dim)]
  transfers between devices with their start and end apart: 6 -> 5, of which waited for: 6 -> 5; matrix products, arithmetic and copies ran while one was open for 0% -> 0% of each run, Pallas kernels for 0% -> 0%
where the time goes in v1:
time: 388 us; the launch traced here: 387 us
  blocking collectives  157 us (40%)
  waiting for transfers between devices  151 us (39%)
  starting transfers between devices  23 us (6%)
  matrix products  20.1 us (5%)
  local copies, waits for them, and re-layouts  18.9 us (5%)
  between operations  13.7 us (4%)
    all_to_all x1, blocking collectives, shards(): lax.all_to_all(jnp.stack([arrived] * lax.axis_size(DEV)), DEV, 0, 0)  99 us
    reduce_scatter x2, waiting for transfers between devices, sum_by_axis(): total = lax.psum_scatter(total, axis, scatter_dimension=0, tiled=True)  84.5 us
    all_to_all x1, waiting for transfers between devices, sent_to_all(): lax.all_to_all(jnp.broadcast_to(shard[None], (peers, *shard.shape)), axis...  48.6 us
    all_gather x1, blocking collectives, side_by_side(): lax.all_gather(both, axis, axis=dim, tiled=True)  26 us
    all_to_all x1, blocking collectives, sent_to_all(): lax.all_to_all(jnp.broadcast_to(shard[None], (peers, *shard.shape)), axis...  18.2 us
    all_to_all x1, blocking collectives, shards(): lax.all_to_all(outgoing, 'grp', split_axis=0, concat_axis=0, tiled=True)  14.3 us
    all_to_all x1, starting transfers between devices, shards(): lax.all_to_all(summed.astype(jnp.bfloat16).reshape(experts, slot_cap, mod...  12.4 us
    dot_general x1, matrix products, shards(): jnp.dot(hidden, down_weight[0], preferred_element_type=jnp.float32)  9.1 us
  transfers between devices with their start and end apart: 5, of which 5 were waited for; matrix products, arithmetic and copies ran while one was open for 0% of the time, Pallas kernels for 0%

profile of v1, /device:TPU:1, one launch (start us, length us, event | category | flops | bytes accessed | tf_op | source)
XLA Modules:
  0.0 387.4 jit_solution(4845573770387338301)
XLA Ops:
  6.6 0.9 negate_bitcast_fusion
  8.7 0.9 copy.73
  10.4 1.0 convolution_convert_fusion.2
  11.6 26.0 %all_gather.3 = bf16[16,2,8193]{2,1,0:T(2,128)(2,1)S(1)} all-gather(bf16[1,2,8193]{2,1,0:T(2,128)(2,1)S(1)} %pad_maximum_fusion), channel_id=1, replica_groups=mesh['grp'=16,'dev_0'=4,'dev_1'=8] {'grp'}, dimensions={0}, use_global_device_ids=true | all-gather | bytes 557124 | tf_op jit(solution)/shard_map/all_gather | solution.py:16
  39.2 1.1 fusion.56
  42.0 18.2 %all_to_all.39 = f32[32,1,256]{2,1,0:T(1,128)S(1)} all-to-all(f32[32,1,256]{2,1,0:T(1,128)S(1)} %broadcast_in_dim.80), channel_id=1, replica_groups=mesh['grp'=16,'dev_0'=4,'dev_1'=8] {'dev_0','dev_1'}, dimensions={0} | all-to-all | bytes 65536 | tf_op jit(solution)/shard_map/all_to_all | solution.py:26
  60.5 1.6 broadcast_in_dim.81
  62.1 4.1 %all-to-all-start.1 = ((bf16[32,256,128]{1,2,0:T(8,128)(2,1)}), bf16[32,256,128]{1,2,0:T(8,128)(2,1)S(1)}, u32[]{:S(2)}, u32[]{:S(2)}) async-start(bf16[32,256,128]{1,2,0:T(8,128)(2,1)} %broadcast_in_dim.81), calls=%async_computation.1 | async-start | bytes 4194304 | tf_op jit(solution)/shard_map/all_to_all | solution.py:26
  66.9 48.6 %all-to-all-done.1 = bf16[32,256,128]{1,2,0:T(8,128)(2,1)S(1)} async-done(((bf16[32,256,128]{1,2,0:T(8,128)(2,1)}), bf16[32,256,128]{1,2,0:T(8,128)(2,1)S(1)}, u32[]{:S(2)}, u32[]{:S(2)}) %all-to-all-start.1) | async-done | bytes 2097184 | tf_op jit(solution)/shard_map/all_to_all | solution.py:26
  115.5 1.5 convolution_convert_fusion.3
  117.9 6.4 %all-to-all-start.2 = ((bf16[32,2,256]{2,1,0:T(2,128)(2,1)}), bf16[32,2,256]{2,1,0:T(2,128)(2,1)S(1)}, u32[]{:S(2)}, u32[]{:S(2)}) async-start(bf16[32,2,256]{2,1,0:T(2,128)(2,1)} %reshape.258), calls=%async_computation.2 | async-start | bytes 65536 | tf_op jit(solution)/shard_map/all_to_all | solution.py:152
  124.4 8.6 %all-to-all-done.2 = bf16[32,2,256]{2,1,0:T(2,128)(2,1)S(1)} async-done(((bf16[32,2,256]{2,1,0:T(2,128)(2,1)}), bf16[32,2,256]{2,1,0:T(2,128)(2,1)S(1)}, u32[]{:S(2)}, u32[]{:S(2)}) %all-to-all-start.2) | async-done | bytes 32800 | tf_op jit(solution)/shard_map/all_to_all | solution.py:152
  133.8 14.3 %all_to_all.40 = bf16[16,2,2048]{2,1,0:T(2,128)(2,1)S(1)} all-to-all(bf16[16,2,2048]{2,1,0:T(2,128)(2,1)S(1)} %reshape.247), channel_id=1, replica_groups=mesh['grp'=16,'dev_0'=4,'dev_1'=8] {'grp'}, dimensions={0} | all-to-all | bytes 262144 | tf_op jit(solution)/shard_map/all_to_all | solution.py:168
  148.1 3.8 stack.2
  151.9 99.0 %all_to_all.41 = bf16[32,16,2,2048]{3,2,1,0:T(2,128)(2,1)} all-to-all(bf16[32,16,2,2048]{3,2,1,0:T(2,128)(2,1)S(1)} %stack.2), channel_id=1, replica_groups=mesh['grp'=16,'dev_0'=4,'dev_1'=8] {'dev_0','dev_1'}, dimensions={0} | all-to-all | bytes 8388608 | tf_op jit(solution)/shard_map/all_to_all | solution.py:170
  250.9 7.3 %reshape_reshape.3 = bf16[1024,2048]{1,0:T(8,128)(2,1)} reshape(bf16[32,16,2,2048]{3,2,1,0:T(2,128)(2,1)} %all_to_all.41) | data formatting | bytes 8388608 | tf_op jit(solution)/shard_map/reshape;reshape | solution.py:171
  258.2 4.5 %fusion.8 = f32[1024,256]{1,0:T(8,128)} fusion(bf16[1024,2048]{1,0:T(8,128)(2,1)} %reshape_reshape.3, bf16[1,2048,256]{2,1,0:T(8,128)(2,1)S(1)} %copy-done.8), kind=kOutput, calls=%fused_computation.15 | convolution fusion | flops 1073741824 | bytes 6291456 | tf_op jit(solution)/shard_map/dot_general | solution.py:172
  262.7 9.1 %convolution_convert_fusion = bf16[1024,2048]{1,0:T(8,128)(2,1)} fusion(bf16[1024,2048]{1,0:T(8,128)(2,1)} %reshape_reshape.3, bf16[1,256,2048]{2,1,0:T(8,128)(2,1)S(1)} %copy-done, bf16[1,2048,256]{2,1,0:T(8,128)(2,1)} %param.30, f32[1024,256]{1,0:T(8,128)} %fusion.8), kind=kOutput, calls=%fused_computation | convolution fusion | flops 2151153664 | bytes 11534336 | tf_op jit(solution)/shard_map/dot_general | solution.py:175
  271.9 45.0 %reduce-scatter.3.cloned.1.call-done = bf16[256,2048]{1,0:T(8,128)(2,1)} async-done(((bf16[1024,2048]{1,0:T(8,128)(2,1)}), bf16[256,2048]{1,0:T(8,128)(2,1)}) %reduce-scatter.3.cloned.1.call-update) | async-done | bytes 1048592 | tf_op jit(solution)/shard_map/reduce_scatter | solution.py:49
  317.0 39.4 %reduce-scatter.5.cloned.1.call-done = bf16[32,2048]{1,0:T(8,128)(2,1)} async-done(((bf16[256,2048]{1,0:T(8,128)(2,1)}), bf16[32,2048]{1,0:T(8,128)(2,1)}) %reduce-scatter.5.cloned.1.call-update) | async-done | bytes 131088 | tf_op jit(solution)/shard_map/reduce_scatter | solution.py:49
  356.4 1.6 reshape.248
  358.1 12.4 %all-to-all-start.5 = ((bf16[16,2,2048]{2,1,0:T(2,128)(2,1)}), bf16[16,2,2048]{2,1,0:T(2,128)(2,1)S(1)}, u32[]{:S(2)}, u32[]{:S(2)}) async-start(bf16[16,2,2048]{2,1,0:T(2,128)(2,1)} %reshape.248), calls=%async_computation.7 | async-start | bytes 262144 | tf_op jit(solution)/shard_map/all_to_all | solution.py:176
  370.9 8.8 %all-to-all-done.5 = bf16[16,2,2048]{2,1,0:T(2,128)(2,1)S(1)} async-done(((bf16[16,2,2048]{2,1,0:T(2,128)(2,1)}), bf16[16,2,2048]{2,1,0:T(2,128)(2,1)S(1)}, u32[]{:S(2)}, u32[]{:S(2)}) %all-to-all-start.5) | async-done | bytes 131104 | tf_op jit(solution)/shard_map/all_to_all | solution.py:176
  379.7 0.9 fusion
  (83 shorter events, 8.6 us)
Async XLA Ops:
  6.5 256.1 %copy-start = (bf16[1,256,2048]{2,1,0:T(8,128)(2,1)S(1)}, bf16[1,256,2048]{2,1,0:T(8,128)(2,1)}, u32[]{:S(2)}) copy-start(bf16[1,256,2048]{2,1,0:T(8,128)(2,1)} %param.31) | copy-start | bytes 3145732
  6.5 34.5 %copy-start.5 = (f32[256,2]{0,1:T(2,128)S(1)}, f32[256,2]{0,1:T(2,128)}, u32[]{:S(2)}) copy-start(f32[256,2]{0,1:T(2,128)} %param.18) | copy-start | bytes 6148
  6.5 34.3 %copy-start.2 = (bf16[256,128]{1,0:T(8,128)(2,1)S(1)}, bf16[256,128]{1,0:T(8,128)(2,1)}, u32[]{:S(2)}) copy-start(bf16[256,128]{1,0:T(8,128)(2,1)} %param.21) | copy-start | bytes 196612
  6.5 34.5 %copy-start.10 = (f32[2]{0:T(128)S(1)}, f32[2]{0:T(128)}, u32[]{:S(2)}) copy-start(f32[2]{0:T(128)} %param.22) | copy-start | bytes 28
  6.5 35.3 %copy-start.1 = (bf16[256,128]{1,0:T(8,128)(2,1)S(1)}, bf16[256,128]{1,0:T(8,128)(2,1)}, u32[]{:S(2)}) copy-start(bf16[256,128]{1,0:T(8,128)(2,1)} %param.17) | copy-start | bytes 196612
  6.5 53.7 %copy-start.7 = (f32[128]{0:T(128)S(1)}, f32[128]{0:T(128)}, u32[]{:S(2)}) copy-start(f32[128]{0:T(128)} %param.23) | copy-start | bytes 1540
  41.1 25.2 %copy-start.6 = (s32[8,2]{0,1:T(2,128)S(1)}, s32[8,2]{0,1:T(2,128)}, u32[]{:S(2)}) copy-start(s32[8,2]{0,1:T(2,128)} %param.28) | copy-start | bytes 196
  62.1 71.2 %copy-start.3 = (bf16[8,2048]{1,0:T(8,128)(2,1)S(1)}, bf16[8,2048]{1,0:T(8,128)(2,1)}, u32[]{:S(2)}) copy-start(bf16[8,2048]{1,0:T(8,128)(2,1)} %param.25) | copy-start | bytes 98308
  62.1 71.4 %copy-start.4 = (f32[2048]{0:T(1024)S(1)}, f32[2048]{0:T(1024)}, u32[]{:S(2)}) copy-start(f32[2048]{0:T(1024)} %param.26) | copy-start | bytes 24580
  62.1 53.4 %all-to-all-start.1 = ((bf16[32,256,128]{1,2,0:T(8,128)(2,1)}), bf16[32,256,128]{1,2,0:T(8,128)(2,1)S(1)}, u32[]{:S(2)}, u32[]{:S(2)}) async-start(bf16[32,256,128]{1,2,0:T(8,128)(2,1)} %broadcast_in_dim.81), calls=%async_computation.1 | async-start | bytes 4194304 | tf_op jit(solution)/shard_map/all_to_all | solution.py:26
  117.9 15.2 %all-to-all-start.2 = ((bf16[32,2,256]{2,1,0:T(2,128)(2,1)}), bf16[32,2,256]{2,1,0:T(2,128)(2,1)S(1)}, u32[]{:S(2)}, u32[]{:S(2)}) async-start(bf16[32,2,256]{2,1,0:T(2,128)(2,1)} %reshape.258), calls=%async_computation.2 | async-start | bytes 65536 | tf_op jit(solution)/shard_map/all_to_all | solution.py:152
  124.3 192.6 %reduce-scatter.3.cloned.1.call-start = ((), (), s32[]{:S(2)}) async-start(), calls=%async_computation.8 | async-start | bytes 5242880 | tf_op jit(solution)/shard_map/reduce_scatter | solution.py:49
  250.9 7.3 %copy-start.8 = (bf16[1,2048,256]{2,1,0:T(8,128)(2,1)S(1)}, bf16[1,2048,256]{2,1,0:T(8,128)(2,1)}, u32[]{:S(2)}) copy-start(bf16[1,2048,256]{2,1,0:T(8,128)(2,1)} %param.29) | copy-start | bytes 3145732
  271.8 98.7 %copy-start.9 = (f32[2048,16]{0,1:T(8,128)S(1)}, f32[2048,16]{0,1:T(8,128)}, u32[]{:S(2)}) copy-start(f32[2048,16]{0,1:T(8,128)} %param.27) | copy-start | bytes 393220
  271.8 84.6 %reduce-scatter.5.cloned.1.call-start = ((), (), s32[]{:S(2)}) async-start(), calls=%async_computation.9 | async-start | bytes 1179648 | tf_op jit(solution)/shard_map/reduce_scatter | solution.py:49
  358.1 21.6 %all-to-all-start.5 = ((bf16[16,2,2048]{2,1,0:T(2,128)(2,1)}), bf16[16,2,2048]{2,1,0:T(2,128)(2,1)S(1)}, u32[]{:S(2)}, u32[]{:S(2)}) async-start(bf16[16,2,2048]{2,1,0:T(2,128)(2,1)} %reshape.248), calls=%async_computation.7 | async-start | bytes 262144 | tf_op jit(solution)/shard_map/all_to_all | solution.py:176
Sparse Core Ops, SparseCore 0:
  271.9 44.9 reduce-scatter.2
  320.0 36.4 reduce-scatter.4
